TPU v7x, 256 devices: a whole 4x4x8 slice. The times are simulated.
256 devices in a mesh: people: 2 (over x_hi), tm: 64 (over z, y, core), type: 2 (over x_lo).
Axes of the slice: x: 4 (x_hi: 2, x_lo: 2; x = x_hi * 2 + x_lo), y: 4, z: 8, core: 2. Of those that a mesh axis runs over, the one named last changes fastest.
Arguments:
- features: bfloat16 [3, 2, 16384], P(None, 'people', 'tm'), may hold values from -6 to 6
- wear: int32 [2, 16384], P('people', 'tm'), may hold values 0 or 1
- rec_start: int32 [2], P('people'), may hold values from 0 to 255
- rec_end: int32 [2], P('people'), may hold values from 16129 to 16384
- conv_first: bfloat16 [3, 3, 128], replicated, may hold values from -2 to 2
- conv_second: bfloat16 [3, 128, 128], replicated, may hold values from -0.3125 to 0.3125
- emit_weight: bfloat16 [128, 512], P(None, 'type'), may hold values from -0.5 to 0.5
- leave: float32 [8, 64], P('type'), may hold values from 0.002 to 0.5
- jump: float32 [8, 64, 64], P('type'), may hold values from -6 to 6
- init_logits: float32 [8, 64], P('type'), may hold values from -6 to 6
- type_prior: float32 [8], replicated, may hold values from -4 to 4
Outputs:
- loglik_rate: float32 [2, 8], P('people', 'type')
- type_post: float32 [2, 8], P('people', 'type')
- occupancy: float32 [8, 64], P('type')
- filtered: float32 [2, 16384, 8, 64], P('people', 'tm', 'type')
All inputs are finite; a program needn't handle non-finite values. No bound on the sum of `wear` on one device may be relied on, other than what follows from the above.
Results may differ from a plain program's by a relative error of at most 0.0085.
Values may be sent and summed in bfloat16 or wider, within the bound.
No kernel may reach another device: no remote copies, remote signals or barrier semaphores. Data moves between devices by JAX's collectives and lax.ppermute only.
A program may use at most 64 MiB of HBM per device.

v0:
```python
import jax
import jax.numpy as jnp
from jax import lax
from jax.sharding import PartitionSpec as P

HIGH = lax.Precision.HIGHEST


def padded(block, sides, width):
    for axis, dim in sides:
        count = lax.axis_size(axis)
        forward = [(i, i + 1) for i in range(count - 1)]
        backward = [(target, source) for source, target in forward]
        low = lax.ppermute(
            lax.slice_in_dim(block, block.shape[dim] - width, None, axis=dim), axis, forward
        )
        high = lax.ppermute(lax.slice_in_dim(block, 0, width, axis=dim), axis, backward)
        block = jnp.concatenate([low, block, high], axis=dim)
    return block


def prefix(shard, axis, combine, identity):
    size, mine = (lax.axis_size(axis), lax.axis_index(axis))
    everything = jax.tree.map(
        lambda part, kind: lax.all_gather(part.astype(kind), axis),
        shard,
        (jnp.bfloat16, jnp.bfloat16),
    )
    start = jax.tree.map(
        lambda part, zero: jnp.broadcast_to(jnp.asarray(zero, part.dtype), part.shape),
        shard,
        identity,
    )

    def turn(k, before):
        reached = k < mine
        new = combine(
            before, jax.tree.map(lambda part, own: part[k].astype(own.dtype), everything, shard)
        )
        return jax.tree.map(lambda a, b: jnp.where(reached, a, b), new, before)

    return lax.fori_loop(0, size, turn, start)


def chain_join(earlier, later):
    left, left_log = earlier
    right, right_log = later
    joined = jnp.einsum("...ij,...jk->...ik", left, right, precision=HIGH)
    scale = jnp.sum(joined, axis=(-2, -1)) / joined.shape[-1]
    return (joined / scale[..., None, None], left_log + right_log + jnp.log(scale))


def chain_product(mats, logs):
    while mats.shape[0] > 1:
        half = mats.shape[0] // 2
        joined, joined_log = chain_join(
            (mats[0 : 2 * half : 2], logs[0 : 2 * half : 2]),
            (mats[1 : 2 * half : 2], logs[1 : 2 * half : 2]),
        )
        mats, logs = (joined, joined_log)
    return (mats[0], logs[0])


def on_device(
    features,
    wear,
    rec_start,
    rec_end,
    conv_first,
    conv_second,
    emit_weight,
    leave,
    jump,
    init_logits,
    type_prior,
):
    persons = features.shape[1]
    span = features.shape[2]
    kinds = jump.shape[0]
    states = jump.shape[-1]
    tm_index = lax.axis_index("tm")
    type_index = lax.axis_index("type")
    total_epochs = span * lax.axis_size("tm")
    extended = padded(features, (("tm", 2),), 5)
    first = jnp.zeros((persons, span + 8, conv_first.shape[2]), jnp.float32)
    for tap in range(3):
        first = first + jnp.einsum(
            "ipt,ic->ptc",
            extended[:, :, tap : tap + span + 8],
            conv_first[tap],
            preferred_element_type=jnp.float32,
        )
    wide_pos = tm_index * span - 4 + jnp.arange(span + 8, dtype=jnp.int32)
    inside = (wide_pos >= 0) & (wide_pos < total_epochs)
    first = jnp.where(inside[None, :, None], jax.nn.silu(first), 0.0).astype(jnp.bfloat16)
    second = jnp.zeros((persons, span, conv_second.shape[2]), jnp.float32)
    for tap in range(3):
        second = second + jnp.einsum(
            "ptc,cd->ptd",
            first[:, 4 * tap : 4 * tap + span],
            conv_second[tap],
            preferred_element_type=jnp.float32,
        )
    second = jax.nn.silu(second).astype(jnp.bfloat16)
    logits = jnp.einsum("ptc,cm->ptm", second, emit_weight, preferred_element_type=jnp.float32)
    probs = jnp.exp(jax.nn.log_softmax(logits.reshape(persons, span, kinds, states), axis=-1))
    positions = tm_index * span + jnp.arange(span, dtype=jnp.int32)
    observed = (
        (wear > 0)
        & (positions[None, :] >= rec_start[:, None])
        & (positions[None, :] < rec_end[:, None])
    )
    emis = jnp.where(observed[:, :, None, None], probs, jnp.float32(1.0))
    observed_f = observed.astype(jnp.float32)
    eye_small = jnp.eye(states, dtype=jnp.float32)
    trans = (1.0 - leave)[..., None] * eye_small + leave[..., None] * jax.nn.softmax(jump, axis=-1)
    start = jax.nn.softmax(init_logits, axis=-1)
    start_all = jnp.broadcast_to(start, (persons, kinds, states))
    group = span // 16
    emis_blocks = jnp.transpose(emis.reshape(persons, 16, group, kinds, states), (1, 2, 0, 3, 4))
    eye_all = jnp.broadcast_to(eye_small, (persons, kinds, states, states))
    zero_logs = jnp.zeros((persons, kinds), jnp.float32)

    def block_leaves(block):
        return trans[None, None] * block[..., None, :]

    def pass_one(carry, block):
        leaves = block_leaves(block)
        product = chain_product(leaves, jnp.zeros(leaves.shape[:3], jnp.float32))
        return (chain_join(carry, product), None)

    (stretch, stretch_log), _ = lax.scan(pass_one, (eye_all, zero_logs), emis_blocks)
    before, before_log = prefix((stretch, stretch_log), "tm", chain_join, (eye_all, zero_logs))
    vec = jnp.einsum("pki,pkij->pkj", start_all, before, precision=HIGH)
    vec_total = jnp.sum(vec, axis=-1)
    alpha_in = vec / vec_total[..., None]
    log_in = before_log + jnp.log(vec_total)

    def advance(carry, inputs):
        alpha_now, log_now, occupied = carry
        emis_now, mask_now = inputs
        pred = jnp.einsum("pki,kij->pkj", alpha_now, trans, precision=HIGH)
        unnorm = pred * emis_now
        step_total = jnp.sum(unnorm, axis=-1)
        alpha_next = unnorm / step_total[..., None]
        occupied = occupied + mask_now[:, None, None] * alpha_next
        return ((alpha_next, log_now + jnp.log(step_total), occupied), alpha_next)

    zero_occupied = jnp.zeros((persons, kinds, states), jnp.float32)
    (alpha_end, own_log, occupied), history = lax.scan(
        advance,
        (alpha_in, zero_logs, zero_occupied),
        (jnp.transpose(emis, (1, 0, 2, 3)), observed_f.T),
    )
    filtered = jnp.transpose(history, (1, 0, 2, 3))
    contribution = log_in + own_log - log_in
    summed = lax.psum(contribution, "tm")
    full = lax.all_gather(summed, "type", axis=1, tiled=True)
    rate_full = full / total_epochs
    post_full = jax.nn.softmax(type_prior[None, :] + 8.0 * rate_full, axis=-1)
    offset = type_index * kinds
    rate_own = lax.dynamic_slice(rate_full, (jnp.int32(0), offset), (persons, kinds))
    post_own = lax.dynamic_slice(post_full, (jnp.int32(0), offset), (persons, kinds))
    numer = jnp.einsum("pk,pks->ks", post_own, occupied, precision=HIGH)
    denom = jnp.einsum("pk,p->k", post_own, jnp.sum(observed_f, axis=1), precision=HIGH)
    numer, denom = lax.psum((numer, denom), ("people", "tm"))
    occupancy = numer / denom[:, None]
    return (rate_own, post_own, occupancy, filtered)


def solution(mesh):
    return jax.shard_map(
        on_device,
        mesh=mesh,
        in_specs=(
            P(None, "people", "tm"),
            P("people", "tm"),
            P("people"),
            P("people"),
            P(),
            P(),
            P(None, "type"),
            P("type", None),
            P("type", None, None),
            P("type", None),
            P(),
        ),
        out_specs=(
            P("people", "type"),
            P("people", "type"),
            P("type", None),
            P("people", "tm", "type", None),
        ),
        check_vma=False,
    )
```

profile of v0, /device:TPU:4, one launch (start us, length us, event | category | flops | bytes accessed | tf_op | source)
XLA Modules:
  0.0 1186.7 jit_solution(14869745420775426021)
XLA Ops:
  8.0 1.7 collective-permute-start
  14.6 1.5 fusion.37
  23.1 85.7 %while.46 = (s32[]{:T(128)}, f32[1,4,64,64]{2,3,1,0:T(8,128)S(1)}, f32[1,4]{1,0:T(1,128)S(1)}, f32[4,64,64]{2,1,0:T(8,128)S(1)}, f32[16,16,1,4,64]{4,3,1,2,0:T(4,128)S(1)}, /*index=5*/s32[]{:T(128)}, s32[]{:T(128)}) while((s32[]{:T(128)}, f32[1,4,64,64]{2,3,1,0:T(8,128)S(1)}, f32[1,4]{1,0:T(1,128)S(1)}, ...), condition=%wide.region_10.11_spmd.clone, body=%wide.region_4.0_spmd.clone.sunk | while | flops 202113104 | bytes 6277803 | solution.py:132
  23.3 1.4 fusion.97
  28.7 1.4 fusion.97
  34.1 1.4 fusion.97
  39.4 1.4 fusion.97
  44.8 1.4 fusion.97
  50.1 1.4 fusion.97
  60.9 1.4 fusion.97
  66.2 1.4 fusion.97
  71.6 1.4 fusion.97
  82.3 1.4 fusion.97
  93.0 1.4 fusion.97
  98.4 1.4 fusion.97
  103.7 1.4 fusion.97
  111.5 45.9 %all-gather.2 = bf16[64,1,4]{2,1,0:T(2,128)(2,1)S(1)} all-gather(bf16[1,1,4]{2,1,0:T(2,128)(2,1)S(1)} %convert_bitcast_fusion.1), channel_id=3, replica_groups=mesh['people'=2,'tm'=64,'type'=2] {'tm'}, dimensions={0}, use_global_device_ids=true | all-gather | bytes 520 | tf_op jit(solution)/shard_map/all_gather | solution.py:25
  157.4 1.6 exponential_select_fusion
  159.1 36.1 %all-gather.5.cloned.1.call-done = bf16[64,4,64,64]{3,2,1,0:T(8,128)(2,1)} async-done(((bf16[1,4,64,64]{3,2,1,0:T(8,128)(2,1)}), bf16[64,4,64,64]{3,2,1,0:T(8,128)(2,1)}) %all-gather.5.cloned.1.call-update) | async-done | bytes 2097168 | tf_op jit(solution)/shard_map/all_gather | solution.py:25
  195.2 86.0 %while.47 = (s32[]{:T(128)}, f32[1,4,64,64]{2,3,1,0:T(8,128)S(1)}, f32[1,4]{1,0:T(1,128)S(1)}, s32[]{:T(128)}, bf16[64,1,4,64,64]{4,3,2,0,1:T(8,128)(2,1)}, /*in...) while((s32[]{:T(128)}, f32[1,4,64,64]{2,3,1,0:T(8,128)S(1)}, f32[1,4]{1,0:T(1,128)S(1)}, ...), condition=%wide.region_13.14_spmd.clone, body=%wide.region_11.13_spmd.clone.sunk | while | flops 12632092 | bytes 393958 | solution.py:42
  281.7 438.0 %while.48 = (s32[]{:T(128)}, f32[1,4,64]{2,1,0:T(4,128)S(1)}, f32[1,4]{1,0:T(1,128)S(1)}, f32[1,4,64]{2,1,0:T(4,128)S(1)}, f32[256,1,4,64]{3,2,1,0:T(4,128)S(1)}...) while((s32[]{:T(128)}, f32[1,4,64]{2,1,0:T(4,128)S(1)}, ...), condition=%wide.region_19.20_spmd.clone, body=%wide.region_17.19_spmd.clone.sunk | while | flops 198407 | bytes 81608 | solution.py:150
  719.7 126.0 %psum.21 = f32[1,4]{1,0:T(1,128)S(1)} all-reduce(f32[1,4]{1,0:T(1,128)S(1)} %add_subtract_fusion), channel_id=1, replica_groups=mesh['people'=2,'tm'=64,'type'=2] {'tm'}, use_global_device_ids=true, to_apply=%region_20.21 | all-reduce | flops 4 | bytes 32 | tf_op jit(solution)/shard_map/psum | solution.py:157
  846.8 4.9 all-reduce
  855.5 323.7 %all-reduce.1 = (f32[4,64]{1,0:T(4,128)S(1)}, f32[4]{0:T(128)S(1)}) all-reduce(f32[4,64]{1,0:T(4,128)S(1)} %bitcast_multiply_fusion.1, f32[4]{0:T(128)S(1)} %get-tuple-element.317), channel_id=1, replica_groups=mesh['people'=2,'tm'=64,'type'=2] {'people','tm'}, use_global_device_ids=true, to_apply=%region_23.24 | all-reduce | flops 260 | bytes 2080 | tf_op jit(solution)/shard_map/psum | solution.py:166
  (2294 shorter events, 601.7 us)
Async XLA Ops:
  7.2 13.7 %copy-start = (bf16[128,256]{1,0:T(8,128)(2,1)S(1)}, bf16[128,256]{1,0:T(8,128)(2,1)}, u32[]{:S(2)}) copy-start(bf16[128,256]{1,0:T(8,128)(2,1)} %param.23) | copy-start | bytes 196612
  7.2 13.5 %copy-start.1 = (bf16[3,128,128]{2,1,0:T(8,128)(2,1)S(1)}, bf16[3,128,128]{2,1,0:T(8,128)(2,1)}, u32[]{:S(2)}) copy-start(bf16[3,128,128]{2,1,0:T(8,128)(2,1)} %param.22) | copy-start | bytes 294916
  7.2 187.9 %all-gather.5.cloned.1.call-start = ((), (), s32[]{:S(2)}) async-start(), calls=%async_computation | async-start | bytes 4259840 | tf_op jit(solution)/shard_map/all_gather | solution.py:25
  8.0 8.1 collective-permute-start
  9.8 6.4 collective-permute-start.1
  23.0 86.6 %copy-start.2 = (f32[4,64]{1,0:T(4,128)S(1)}, f32[4,64]{1,0:T(4,128)}, u32[]{:S(2)}) copy-start(f32[4,64]{1,0:T(4,128)} %param.26) | copy-start | bytes 3076
  23.0 86.7 %copy-start.5 = (u32[256]{0:T(256)S(1)}, u32[256]{0:T(256)}, u32[]{:S(2)}) copy-start(u32[256]{0:T(256)} %constant.125) | copy-start | bytes 3076
  195.1 656.5 %copy-start.4 = (f32[8]{0:T(128)S(1)}, f32[8]{0:T(128)}, u32[]{:S(2)}) copy-start(f32[8]{0:T(128)} %param.27) | copy-start | bytes 100
  855.4 324.4 %copy-start.3 = (f32[1,4]{1,0:T(1,128)}, f32[1,4]{1,0:T(1,128)S(1)}, u32[]{:S(2)}) copy-start(f32[1,4]{1,0:T(1,128)S(1)} %get-tuple-element.318) | copy-start | bytes 52
Sparse Core Ops, SparseCore 0:
  109.7 85.4 all-gather.4
where the time goes:
time: 1190 us
  blocking collectives  501 us (42%)
  other arithmetic  258 us (22%)
  matrix products  195 us (16%)
  local copies, waits for them, and re-layouts  168 us (14%)
  waiting for transfers between devices  36.1 us (3%)
  between operations  16.3 us (1%)
    psum x1, blocking collectives, on_device(): numer, denom = lax.psum((numer, denom), ('people', 'tm'))  324 us
    add x256, other arithmetic, advance(): occupied = occupied + mask_now[:, None, None] * alpha_next  168 us
    dynamic_slice x256, local copies, waits for them, and re-layouts, on_device(): lax.scan(advance, (alpha_in, zero_logs, zero_occupied), (jnp.transpose(em...  151 us
    dot_general x144, matrix products, chain_join(): joined = jnp.einsum('...ij,...jk->...ik', left, right, precision=HIGH)  134 us
    psum x1, blocking collectives, on_device(): summed = lax.psum(contribution, 'tm')  126 us
    dot_general x256, matrix products, advance(): pred = jnp.einsum('pki,kij->pkj', alpha_now, trans, precision=HIGH)  57.1 us
    all_gather x1, blocking collectives, prefix(): lax.all_gather(part.astype(kind), axis)  45.9 us
    all_gather x1, waiting for transfers between devices, prefix(): lax.all_gather(part.astype(kind), axis)  36.1 us
  transfers between devices with their start and end apart: 3, of which 1 were waited for; matrix products, arithmetic and copies ran while one was open for 1% of the time, Pallas kernels for 0%

commit v1 on v0

v1 whole, which is shorter than its diff:
```python
import jax
import jax.numpy as jnp
from jax import lax
from jax.sharding import PartitionSpec as P

HIGHEST = lax.Precision.HIGHEST
HIGH = lax.Precision.HIGH


def padded(block, sides, width):
    for axis, dim in sides:
        count = lax.axis_size(axis)
        forward = [(i, i + 1) for i in range(count - 1)]
        backward = [(target, source) for source, target in forward]
        low = lax.ppermute(
            lax.slice_in_dim(block, block.shape[dim] - width, None, axis=dim), axis, forward
        )
        high = lax.ppermute(lax.slice_in_dim(block, 0, width, axis=dim), axis, backward)
        block = jnp.concatenate([low, block, high], axis=dim)
    return block


def norm_mat(m):
    return m / jnp.sum(m, axis=(-2, -1), keepdims=True)


def norm_vec(v):
    return v / jnp.sum(v, axis=-1, keepdims=True)


def mat_mat(a, b):
    return jnp.einsum("...im,...ml->...il", a, b, precision=HIGH)


def shift_in(x, axis, step, fill):
    count = lax.axis_size(axis)
    if step >= count:
        return jnp.broadcast_to(fill, x.shape)
    moved = lax.ppermute(x, axis, [(i, i + step) for i in range(count - step)])
    return jnp.where(lax.axis_index(axis) >= step, moved, fill)


def exclusive_scan(mats, axis):
    count = lax.axis_size(axis)
    eye = jnp.eye(mats.shape[-1], dtype=mats.dtype)
    one = shift_in(mats, axis, 1, eye)
    two = shift_in(mats, axis, 2, eye)
    acc = norm_mat(mat_mat(two, one))
    step = 2
    while step < count:
        acc = norm_mat(mat_mat(shift_in(acc, axis, step, eye), acc))
        step *= 2
    return acc


def butterfly_sum(x, axes):
    for axis in axes:
        count = lax.axis_size(axis)
        bit = 1
        while bit < count:
            x = x + lax.ppermute(x, axis, [(i, i ^ bit) for i in range(count)])
            bit *= 2
    return x


def on_device(
    features,
    wear,
    rec_start,
    rec_end,
    conv_first,
    conv_second,
    emit_weight,
    leave,
    jump,
    init_logits,
    type_prior,
):
    persons = features.shape[1]
    span = features.shape[2]
    kinds = jump.shape[0]
    states = jump.shape[-1]
    tm_index = lax.axis_index("tm")
    type_index = lax.axis_index("type")
    people_index = lax.axis_index("people")
    total_epochs = span * lax.axis_size("tm")
    extended = padded(features, (("tm", 2),), 5)
    first = jnp.zeros((persons, span + 8, conv_first.shape[2]), jnp.float32)
    for tap in range(3):
        first = first + jnp.einsum(
            "ipt,ic->ptc",
            extended[:, :, tap : tap + span + 8],
            conv_first[tap],
            preferred_element_type=jnp.float32,
        )
    wide_pos = tm_index * span - 4 + jnp.arange(span + 8, dtype=jnp.int32)
    inside = (wide_pos >= 0) & (wide_pos < total_epochs)
    first = jnp.where(inside[None, :, None], jax.nn.silu(first), 0.0).astype(jnp.bfloat16)
    second = jnp.zeros((persons, span, conv_second.shape[2]), jnp.float32)
    for tap in range(3):
        second = second + jnp.einsum(
            "ptc,cd->ptd",
            first[:, 4 * tap : 4 * tap + span],
            conv_second[tap],
            preferred_element_type=jnp.float32,
        )
    second = jax.nn.silu(second).astype(jnp.bfloat16)
    logits = jnp.einsum("ptc,cm->ptm", second, emit_weight, preferred_element_type=jnp.float32)
    probs = jnp.exp(jax.nn.log_softmax(logits.reshape(persons, span, kinds, states), axis=-1))
    positions = tm_index * span + jnp.arange(span, dtype=jnp.int32)
    observed = (
        (wear > 0)
        & (positions[None, :] >= rec_start[:, None])
        & (positions[None, :] < rec_end[:, None])
    )
    emis = jnp.where(observed[:, :, None, None], probs, jnp.float32(1.0))
    observed_f = observed.astype(jnp.float32)
    eye_small = jnp.eye(states, dtype=jnp.float32)
    trans = (1.0 - leave)[..., None] * eye_small + leave[..., None] * jax.nn.softmax(jump, axis=-1)
    start = jax.nn.softmax(init_logits, axis=-1)

    pairs = emis.reshape(persons, span // 2, 2, kinds, states)
    e_even = pairs[:, :, 0]
    e_odd = pairs[:, :, 1]
    left = trans[None, None] * e_even[:, :, :, None, :]
    level = jnp.einsum("pjkim,kml->pjkil", left, trans, precision=HIGH) * e_odd[:, :, :, None, :]
    levels = [None, norm_mat(level)]
    while levels[-1].shape[1] > 1:
        last = levels[-1]
        halves = last.reshape((persons, last.shape[1] // 2, 2) + last.shape[2:])
        levels.append(norm_mat(mat_mat(halves[:, :, 0], halves[:, :, 1])))
    device_op = levels[-1][:, 0]

    before = exclusive_scan(device_op, "tm")
    alpha_in = norm_vec(jnp.einsum("ki,pkij->pkj", start, before, precision=HIGHEST))

    entry = alpha_in[:, None]
    for depth in range(len(levels) - 1, 1, -1):
        sibling = levels[depth - 1].reshape(
            (persons, entry.shape[1], 2) + levels[depth - 1].shape[2:]
        )[:, :, 0]
        moved = norm_vec(jnp.einsum("pnki,pnkil->pnkl", entry, sibling, precision=HIGHEST))
        entry = jnp.stack([entry, moved], axis=2).reshape(
            persons, 2 * entry.shape[1], kinds, states
        )
    u = jnp.einsum("pjki,kil->pjkl", entry, trans, precision=HIGHEST) * e_even
    c_even = jnp.sum(u, axis=-1)
    a_even = u / c_even[..., None]
    v = jnp.einsum("pjki,kil->pjkl", a_even, trans, precision=HIGHEST) * e_odd
    c_odd = jnp.sum(v, axis=-1)
    a_odd = v / c_odd[..., None]
    filtered = jnp.stack([a_even, a_odd], axis=2).reshape(persons, span, kinds, states)
    own_log = jnp.sum(jnp.log(c_even), axis=1) + jnp.sum(jnp.log(c_odd), axis=1)
    occupied = jnp.einsum("pt,ptks->pks", observed_f, filtered, precision=HIGHEST)
    count = jnp.sum(observed_f, axis=1)

    halves_n = lax.axis_size("type")
    people_n = lax.axis_size("people") * persons
    row = jnp.concatenate(
        [own_log, occupied.reshape(persons, kinds * states), count[:, None]], axis=1
    )
    person_hot = (
        people_index * persons + jnp.arange(persons)[:, None] == jnp.arange(people_n)[None, :]
    ).astype(jnp.float32)
    half_hot = (type_index == jnp.arange(halves_n)).astype(jnp.float32)
    table = person_hot[:, :, None, None] * half_hot[None, None, :, None] * row[:, None, None, :]
    table = butterfly_sum(jnp.sum(table, axis=0), ("type", "people", "tm"))

    full = table[:, :, :kinds].reshape(people_n, halves_n * kinds)
    rate_full = full / total_epochs
    post_full = jax.nn.softmax(type_prior[None, :] + 8.0 * rate_full, axis=-1)
    offset = type_index * kinds
    mine = people_index * persons
    rate_own = lax.dynamic_slice(rate_full, (mine, offset), (persons, kinds))
    post_own = lax.dynamic_slice(post_full, (mine, offset), (persons, kinds))
    post_type = lax.dynamic_slice(post_full, (jnp.int32(0), offset), (people_n, kinds))
    occ_all = jnp.take(table, type_index, axis=1)[:, kinds : kinds + kinds * states]
    occ_all = occ_all.reshape(people_n, kinds, states)
    cnt_all = jnp.take(table, type_index, axis=1)[:, kinds + kinds * states]
    numer = jnp.einsum("pk,pks->ks", post_type, occ_all, precision=HIGHEST)
    denom = jnp.einsum("pk,p->k", post_type, cnt_all, precision=HIGHEST)
    occupancy = numer / denom[:, None]
    return (rate_own, post_own, occupancy, filtered)


def solution(mesh):
    return jax.shard_map(
        on_device,
        mesh=mesh,
        in_specs=(
            P(None, "people", "tm"),
            P("people", "tm"),
            P("people"),
            P("people"),
            P(),
            P(),
            P(None, "type"),
            P("type", None),
            P("type", None, None),
            P("type", None),
            P(),
        ),
        out_specs=(
            P("people", "type"),
            P("people", "type"),
            P("type", None),
            P("people", "tm", "type", None),
        ),
        check_vma=False,
    )
```

time: 1190 us -> 256 us (0.22)
  blocking collectives: 501 us -> 0 us
  other arithmetic: 258 us -> 21.6 us
  local copies, waits for them, and re-layouts: 168 us -> 23.9 us
  matrix products: 195 us -> 59.7 us
  starting transfers between devices: 3.06 us -> 75.4 us
  waiting for transfers between devices: 36.1 us -> 71.6 us
  between operations: 16.3 us -> 2.6 us
    psum x2 -> x0, blocking collectives: 450 us -> none  [the longest x1 324 us: on_device(): numer, denom = lax.psum((numer, denom), ('people', 'tm'))]
    add x576 -> x10, other arithmetic: 175 us -> 1.25 us  [the longest x1 0.85 us: on_device(): (1.0 - leave)[..., None] * eye_small]
    dynamic_slice x257 -> x4, local copies, waits for them, and re-layouts: 152 us -> 0.84 us  [the longest x1 0.6 us: on_device(): post_own = lax.dynamic_slice(post_full, (mine, offset), (persons, kinds))]
    dot_general x401 -> x27, matrix products: 191 us -> 53.9 us  [the longest x13 22.6 us: mat_mat(): return jnp.einsum('...im,...ml->...il', a, b, precision=HIGH)]
    ppermute x0 -> x15, starting transfers between devices: none -> 72.4 us  [the longest x7 61.8 us: shift_in(): moved = lax.ppermute(x, axis, [(i, i + step) for i in range(count - step)])]
    ppermute x0 -> x15, waiting for transfers between devices: none -> 71.6 us  [the longest x8 60 us: butterfly_sum(): x = x + lax.ppermute(x, axis, [(i, i ^ bit) for i in range(count)])]
    all_gather x1 -> x0, blocking collectives: 45.9 us -> none  [prefix(): lax.all_gather(part.astype(kind), axis)]
    all_gather x1 -> x0, waiting for transfers between devices: 36.1 us -> none  [prefix(): lax.all_gather(part.astype(kind), axis)]
  transfers between devices with their start and end apart: 3 -> 17, of which waited for: 1 -> 14; matrix products, arithmetic and copies ran while one was open for 1% -> 2% of each run, Pallas kernels for 0% -> 0%
where the time goes in v1:
time: 256 us; the launch traced here: 255 us
  starting transfers between devices  75.4 us (29%)
  waiting for transfers between devices  71.6 us (28%)
  matrix products  59.7 us (23%)
  local copies, waits for them, and re-layouts  23.9 us (9%)
  other arithmetic  21.6 us (8%)
  between operations  2.6 us (1%)
    ppermute x7, starting transfers between devices, shift_in(): moved = lax.ppermute(x, axis, [(i, i + step) for i in range(count - step)])  61.8 us
    ppermute x8, waiting for transfers between devices, butterfly_sum(): x = x + lax.ppermute(x, axis, [(i, i ^ bit) for i in range(count)])  60 us
    dot_general x13, matrix products, mat_mat(): return jnp.einsum('...im,...ml->...il', a, b, precision=HIGH)  22.6 us
    dot_general x7, matrix products, on_device(): jnp.einsum('pnki,pnkil->pnkl', entry, sibling, precision=HIGHEST)  22.2 us
    div x1, local copies, waits for them, and re-layouts, norm_mat(): return m / jnp.sum(m, axis=(-2, -1), keepdims=True)  16.2 us
    ppermute x7, waiting for transfers between devices, shift_in(): moved = lax.ppermute(x, axis, [(i, i + step) for i in range(count - step)])  11.6 us
    div x11, other arithmetic, norm_mat(): return m / jnp.sum(m, axis=(-2, -1), keepdims=True)  11.1 us
    ppermute x8, starting transfers between devices, butterfly_sum(): x = x + lax.ppermute(x, axis, [(i, i ^ bit) for i in range(count)])  10.6 us
  transfers between devices with their start and end apart: 17, of which 14 were waited for; matrix products, arithmetic and copies ran while one was open for 2% of the time, Pallas kernels for 0%

profile of v1, /device:TPU:4, one launch (start us, length us, event | category | flops | bytes accessed | tf_op | source)
XLA Modules:
  0.0 254.8 jit_solution(1105410566738748770)
XLA Ops:
  18.1 7.1 %fusion.11 = (f32[128,4]{0,1:T(4,128)S(1)}, f32[4,64,128,64]{2,1,3,0:T(8,128)S(1)}) fusion(f32[128,4,64]{0,2,1:T(8,128)S(1)} %get-tuple-element.29, f32[128,4,64]{0,2,1:T(8,128)S(1)} %get-tuple-element.30, f32[4,64,64]{2,1,0:T(8,128)S(1)} %multiply_add_fusion), kind=kOutput, calls=%fused_computation.14 | convolution fusion | flops 811597312 | bytes 8718336 | tf_op jit(solution)/shard_map/pjkim,kml->pjkil/dot_general | solution.py:126
  25.2 4.3 %fusion.10 = f32[1,128,4,64,64]{1,4,3,2,0:T(8,128)} fusion(f32[4,64,128,64]{2,1,3,0:T(8,128)S(1)} %get-tuple-element.40, f32[128,4]{0,1:T(4,128)S(1)} %get-tuple-element.39, f32[128,4,64]{0,2,1:T(8,128)S(1)} %get-tuple-element.29), kind=kLoop, calls=%fused_computation.13 | loop fusion | flops 4194304 | bytes 16910336 | tf_op jit(solution)/shard_map/div | solution.py:24
  29.5 16.2 %copy.82 = f32[1,128,4,64,64]{4,3,2,1,0:T(8,128)} copy(f32[1,128,4,64,64]{1,4,3,2,0:T(8,128)} %fusion.10) | data formatting | bytes 16777216 | tf_op jit(solution)/shard_map/div | solution.py:24
  45.7 14.2 %fusion.137 = (f32[64,4]{1,0:T(8,128)S(1)}, f32[64,4,64,64]{3,2,1,0:T(8,128)}) fusion(f32[1,64,2,4,64,64]{5,4,3,2,1,0:T(8,128)} %bitcast.367), kind=kOutput, calls=%fused_computation.220 | convolution fusion | flops 403701504 | bytes 12583936 | tf_op jit(solution)/shard_map/...im,...ml->...il/dot_general | solution.py:32
  59.9 4.1 %broadcast_divide_fusion = f32[64,4,64,64]{3,2,1,0:T(8,128)S(1)} fusion(f32[64,4,64,64]{3,2,1,0:T(8,128)} %get-tuple-element.42, f32[64,4]{1,0:T(8,128)S(1)} %get-tuple-element.41), kind=kLoop, calls=%fused_computation.19 | loop fusion | flops 1048576 | bytes 8389632 | tf_op jit(solution)/shard_map/div | solution.py:24
  64.0 3.0 %fusion.138 = (f32[32,4]{1,0:T(8,128)S(1)}, f32[32,4,64,64]{3,2,1,0:T(8,128)S(1)}) fusion(f32[1,32,2,4,64,64]{5,4,3,2,1,0:T(8,128)S(1)} %bitcast.369), kind=kOutput, calls=%fused_computation.221 | convolution fusion | flops 201850752 | bytes 6291968 | tf_op jit(solution)/shard_map/...im,...ml->...il/dot_general | solution.py:32
  73.1 6.7 %collective-permute-start.2 = (f32[1,4,64,64]{3,2,1,0:T(8,128)S(1)}, f32[1,4,64,64]{3,2,1,0:T(8,128)}, u32[]{:S(2)}, u32[]{:S(2)}) collective-permute-start(f32[1,4,64,64]{3,2,1,0:T(8,128)S(1)} %divide_bitcast_fusion.2), channel_id=1, source_target_pairs={{0,4},{2,6},{4,8},{6,10},{8,12},{10,14},{12,16},{14,18},{16,20},{1... | collective-permute-start | bytes 196616 | tf_op jit(solution)/shard_map/ppermute | solution.py:39
  82.8 7.5 %collective-permute-start.4 = (f32[1,4,64,64]{3,2,1,0:T(8,128)S(1)}, f32[1,4,64,64]{3,2,1,0:T(8,128)S(1)}, u32[]{:S(2)}, u32[]{:S(2)}) collective-permute-start(f32[1,4,64,64]{3,2,1,0:T(8,128)S(1)} %fusion.105), channel_id=1, source_target_pairs={{0,4},{2,6},{4,8},{6,10},{8,12},{10,14},{12,16},{14,18},{16,20},{1... | collective-permute-start | bytes 196616 | tf_op jit(solution)/shard_map/ppermute | solution.py:39
  94.0 7.6 %collective-permute-start.5 = (f32[1,4,64,64]{3,2,1,0:T(8,128)}, f32[1,4,64,64]{3,2,1,0:T(8,128)}, u32[]{:S(2)}, u32[]{:S(2)}) collective-permute-start(f32[1,4,64,64]{3,2,1,0:T(8,128)} %fusion.106), channel_id=1, source_target_pairs={{0,8},{2,10},{4,12},{6,14},{8,16},{10,18},{12,20},{14,22},{16,24},... | collective-permute-start | bytes 196616 | tf_op jit(solution)/shard_map/ppermute | solution.py:39
  101.6 2.5 collective-permute-done.5
  104.6 9.8 %collective-permute-start.6 = (f32[1,4,64,64]{3,2,1,0:T(8,128)S(1)}, f32[1,4,64,64]{3,2,1,0:T(8,128)S(1)}, u32[]{:S(2)}, u32[]{:S(2)}) collective-permute-start(f32[1,4,64,64]{3,2,1,0:T(8,128)S(1)} %fusion.107), channel_id=1, source_target_pairs={{0,16},{2,18},{4,20},{6,22},{8,24},{10,26},{12,28},{14,30},{16,32}... | collective-permute-start | bytes 196616 | tf_op jit(solution)/shard_map/ppermute | solution.py:39
  118.0 6.3 %collective-permute-start.7 = (f32[1,4,64,64]{3,2,1,0:T(8,128)}, f32[1,4,64,64]{3,2,1,0:T(8,128)}, u32[]{:S(2)}, u32[]{:S(2)}) collective-permute-start(f32[1,4,64,64]{3,2,1,0:T(8,128)} %fusion.108), channel_id=1, source_target_pairs={{0,32},{2,34},{4,36},{6,38},{8,40},{10,42},{12,44},{14,46},{16,48}... | collective-permute-start | bytes 196616 | tf_op jit(solution)/shard_map/ppermute | solution.py:39
  127.0 21.6 %collective-permute-start.8 = (f32[1,4,64,64]{3,2,1,0:T(8,128)S(1)}, f32[1,4,64,64]{3,2,1,0:T(8,128)S(1)}, u32[]{:S(2)}, u32[]{:S(2)}) collective-permute-start(f32[1,4,64,64]{3,2,1,0:T(8,128)S(1)} %fusion.109), channel_id=1, source_target_pairs={{0,64},{2,66},{4,68},{6,70},{8,72},{10,74},{12,76},{14,78},{16,80}... | collective-permute-start | bytes 196616 | tf_op jit(solution)/shard_map/ppermute | solution.py:39
  157.0 3.5 %fusion.18 = f32[16,4,1,64]{3,2,1,0:T(1,128)S(1)} fusion(f32[1,16,2,4,64,64]{5,4,3,2,1,0:T(8,128)} %bitcast.372, f32[16,4,64,1]{2,0,1,3:T(8,128)S(1)} %bitcast.391), kind=kOutput, calls=%fused_computation.27 | convolution fusion | flops 3145728 | bytes 2129920 | tf_op jit(solution)/shard_map/pnki,pnkil->pnkl/dot_general | solution.py:142
  160.9 5.3 %fusion.16 = f32[32,4,1,64]{3,2,1,0:T(1,128)S(1)} fusion(f32[1,32,2,4,64,64]{5,4,3,2,1,0:T(8,128)} %bitcast.370, f32[32,4,64,1]{2,0,1,3:T(8,128)S(1)} %bitcast.386), kind=kOutput, calls=%fused_computation.22 | convolution fusion | flops 6291456 | bytes 4259840 | tf_op jit(solution)/shard_map/pnki,pnkil->pnkl/dot_general | solution.py:142
  166.8 9.5 %fusion.12 = f32[64,4,1,64]{3,2,1,0:T(1,128)S(1)} fusion(f32[1,64,2,4,64,64]{5,4,3,2,1,0:T(8,128)} %bitcast.368, f32[64,4,64,1]{2,0,1,3:T(8,128)S(1)} %bitcast.381), kind=kOutput, calls=%fused_computation.15 | convolution fusion | flops 12582912 | bytes 8519680 | tf_op jit(solution)/shard_map/pnki,pnkil->pnkl/dot_general | solution.py:142
  181.1 5.3 %collective-permute-done.9 = f32[2,2,261]{0,2,1:T(8,128)S(1)} collective-permute-done((f32[2,2,261]{0,2,1:T(8,128)S(1)}, f32[2,2,261]{0,2,1:T(8,128)S(1)}, u32[]{:S(2)}, u32[]{:S(2)}) %collective-permute-start.9) | collective-permute-done | bytes 4208 | tf_op jit(solution)/shard_map/ppermute | solution.py:61
  187.0 7.5 %collective-permute-done.10 = f32[2,2,261]{0,2,1:T(8,128)S(1)} collective-permute-done((f32[2,2,261]{0,2,1:T(8,128)S(1)}, f32[2,2,261]{0,2,1:T(8,128)S(1)}, u32[]{:S(2)}, u32[]{:S(2)}) %collective-permute-start.10) | collective-permute-done | bytes 4208 | tf_op jit(solution)/shard_map/ppermute | solution.py:61
  196.4 8.5 %collective-permute-done.12 = f32[2,2,261]{0,2,1:T(8,128)S(1)} collective-permute-done((f32[2,2,261]{0,2,1:T(8,128)S(1)}, f32[2,2,261]{0,2,1:T(8,128)S(1)}, u32[]{:S(2)}, u32[]{:S(2)}) %collective-permute-start.12) | collective-permute-done | bytes 4208 | tf_op jit(solution)/shard_map/ppermute | solution.py:61
  205.0 9.2 %collective-permute-done.13 = f32[2,2,261]{0,2,1:T(8,128)S(1)} collective-permute-done((f32[2,2,261]{0,2,1:T(8,128)S(1)}, f32[2,2,261]{0,2,1:T(8,128)S(1)}, u32[]{:S(2)}, u32[]{:S(2)}) %collective-permute-start.13) | collective-permute-done | bytes 4208 | tf_op jit(solution)/shard_map/ppermute | solution.py:61
  216.0 5.5 %collective-permute-done.14 = f32[2,2,261]{0,2,1:T(8,128)S(1)} collective-permute-done((f32[2,2,261]{0,2,1:T(8,128)S(1)}, f32[2,2,261]{0,2,1:T(8,128)S(1)}, u32[]{:S(2)}, u32[]{:S(2)}) %collective-permute-start.14) | collective-permute-done | bytes 4208 | tf_op jit(solution)/shard_map/ppermute | solution.py:61
  221.6 12.3 %collective-permute-done.15 = f32[2,2,261]{0,2,1:T(8,128)S(1)} collective-permute-done((f32[2,2,261]{0,2,1:T(8,128)S(1)}, f32[2,2,261]{0,2,1:T(8,128)S(1)}, u32[]{:S(2)}, u32[]{:S(2)}) %collective-permute-start.15) | collective-permute-done | bytes 4208 | tf_op jit(solution)/shard_map/ppermute | solution.py:61
  233.9 6.5 %collective-permute-start.16 = (f32[2,2,261]{0,2,1:T(8,128)S(1)}, f32[2,2,261]{0,2,1:T(8,128)S(1)}, u32[]{:S(2)}, u32[]{:S(2)}) collective-permute-start(f32[2,2,261]{0,2,1:T(8,128)S(1)} %add.143), channel_id=1, source_target_pairs={{0,64},{2,66},{4,68},{6,70},{8,72},{10,74},{12,76},{14,78},{16,80}... | collective-permute-start | bytes 12536 | tf_op jit(solution)/shard_map/ppermute | solution.py:61
  241.4 10.3 %collective-permute-done.16 = f32[2,2,261]{0,2,1:T(8,128)S(1)} collective-permute-done((f32[2,2,261]{0,2,1:T(8,128)S(1)}, f32[2,2,261]{0,2,1:T(8,128)S(1)}, u32[]{:S(2)}, u32[]{:S(2)}) %collective-permute-start.16) | collective-permute-done | bytes 4208 | tf_op jit(solution)/shard_map/ppermute | solution.py:61
  (158 shorter events, 58.0 us)
Async XLA Ops:
  0.6 14.4 %copy-start = (bf16[128,256]{1,0:T(8,128)(2,1)S(1)}, bf16[128,256]{1,0:T(8,128)(2,1)}, u32[]{:S(2)}) copy-start(bf16[128,256]{1,0:T(8,128)(2,1)} %param.19) | copy-start | bytes 196612
  1.4 8.1 %collective-permute-start = (bf16[3,1,5]{2,0,1:T(4,128)(2,1)S(1)}, bf16[3,1,5]{2,0,1:T(4,128)(2,1)S(1)}, u32[]{:S(2)}, u32[]{:S(2)}) collective-permute-start(bf16[3,1,5]{2,0,1:T(4,128)(2,1)S(1)} %get-tuple-element.33), channel_id=1, source_target_pairs={{0,2},{2,4},{4,6},{6,8},{8,10},{10,12},{12,14},{14,16},{16,18},{18... | collective-permute-start | bytes 98 | tf_op jit(solution)/shard_map/ppermute | solution.py:15
  3.2 6.3 %collective-permute-start.1 = (bf16[3,1,5]{2,0,1:T(4,128)(2,1)S(1)}, bf16[3,1,5]{2,0,1:T(4,128)(2,1)S(1)}, u32[]{:S(2)}, u32[]{:S(2)}) collective-permute-start(bf16[3,1,5]{2,0,1:T(4,128)(2,1)S(1)} %get-tuple-element.34), channel_id=1, source_target_pairs={{2,0},{4,2},{6,4},{8,6},{10,8},{12,10},{14,12},{16,14},{18,16},{20... | collective-permute-start | bytes 98 | tf_op jit(solution)/shard_map/ppermute | solution.py:18
  64.0 3.5 %copy-start.2 = (f32[64,4,64,64]{3,2,1,0:T(8,128)}, f32[64,4,64,64]{3,2,1,0:T(8,128)S(1)}, u32[]{:S(2)}) copy-start(f32[64,4,64,64]{3,2,1,0:T(8,128)S(1)} %broadcast_divide_fusion) | copy-start | bytes 12582916
  67.5 3.0 %copy-start.3 = (f32[32,4,64,64]{3,2,1,0:T(8,128)}, f32[32,4,64,64]{3,2,1,0:T(8,128)S(1)}, u32[]{:S(2)}) copy-start(f32[32,4,64,64]{3,2,1,0:T(8,128)S(1)} %broadcast_divide_fusion.1) | copy-start | bytes 6291460
  68.9 13.1 %copy-start.8 = (f32[4,64]{1,0:T(4,128)S(1)}, f32[4,64]{1,0:T(4,128)}, u32[]{:S(2)}) copy-start(f32[4,64]{1,0:T(4,128)} %param.22) | copy-start | bytes 3076
  73.1 9.0 %collective-permute-start.2 = (f32[1,4,64,64]{3,2,1,0:T(8,128)S(1)}, f32[1,4,64,64]{3,2,1,0:T(8,128)}, u32[]{:S(2)}, u32[]{:S(2)}) collective-permute-start(f32[1,4,64,64]{3,2,1,0:T(8,128)S(1)} %divide_bitcast_fusion.2), channel_id=1, source_target_pairs={{0,4},{2,6},{4,8},{6,10},{8,12},{10,14},{12,16},{14,18},{16,20},{1... | collective-permute-start | bytes 196616 | tf_op jit(solution)/shard_map/ppermute | solution.py:39
  79.7 2.7 %collective-permute-start.3 = (f32[1,4,64,64]{3,2,1,0:T(8,128)S(1)}, f32[1,4,64,64]{3,2,1,0:T(8,128)}, u32[]{:S(2)}, u32[]{:S(2)}) collective-permute-start(f32[1,4,64,64]{3,2,1,0:T(8,128)S(1)} %divide_bitcast_fusion.2), channel_id=1, source_target_pairs={{0,2},{2,4},{4,6},{6,8},{8,10},{10,12},{12,14},{14,16},{16,18},{18... | collective-permute-start | bytes 196616 | tf_op jit(solution)/shard_map/ppermute | solution.py:39
  82.8 10.0 %collective-permute-start.4 = (f32[1,4,64,64]{3,2,1,0:T(8,128)S(1)}, f32[1,4,64,64]{3,2,1,0:T(8,128)S(1)}, u32[]{:S(2)}, u32[]{:S(2)}) collective-permute-start(f32[1,4,64,64]{3,2,1,0:T(8,128)S(1)} %fusion.105), channel_id=1, source_target_pairs={{0,4},{2,6},{4,8},{6,10},{8,12},{10,14},{12,16},{14,18},{16,20},{1... | collective-permute-start | bytes 196616 | tf_op jit(solution)/shard_map/ppermute | solution.py:39
  94.0 10.1 %collective-permute-start.5 = (f32[1,4,64,64]{3,2,1,0:T(8,128)}, f32[1,4,64,64]{3,2,1,0:T(8,128)}, u32[]{:S(2)}, u32[]{:S(2)}) collective-permute-start(f32[1,4,64,64]{3,2,1,0:T(8,128)} %fusion.106), channel_id=1, source_target_pairs={{0,8},{2,10},{4,12},{6,14},{8,16},{10,18},{12,20},{14,22},{16,24},... | collective-permute-start | bytes 196616 | tf_op jit(solution)/shard_map/ppermute | solution.py:39
  104.6 12.4 %collective-permute-start.6 = (f32[1,4,64,64]{3,2,1,0:T(8,128)S(1)}, f32[1,4,64,64]{3,2,1,0:T(8,128)S(1)}, u32[]{:S(2)}, u32[]{:S(2)}) collective-permute-start(f32[1,4,64,64]{3,2,1,0:T(8,128)S(1)} %fusion.107), channel_id=1, source_target_pairs={{0,16},{2,18},{4,20},{6,22},{8,24},{10,26},{12,28},{14,30},{16,32}... | collective-permute-start | bytes 196616 | tf_op jit(solution)/shard_map/ppermute | solution.py:39
  118.0 8.5 %collective-permute-start.7 = (f32[1,4,64,64]{3,2,1,0:T(8,128)}, f32[1,4,64,64]{3,2,1,0:T(8,128)}, u32[]{:S(2)}, u32[]{:S(2)}) collective-permute-start(f32[1,4,64,64]{3,2,1,0:T(8,128)} %fusion.108), channel_id=1, source_target_pairs={{0,32},{2,34},{4,36},{6,38},{8,40},{10,42},{12,44},{14,46},{16,48}... | collective-permute-start | bytes 196616 | tf_op jit(solution)/shard_map/ppermute | solution.py:39
  127.0 24.1 %collective-permute-start.8 = (f32[1,4,64,64]{3,2,1,0:T(8,128)S(1)}, f32[1,4,64,64]{3,2,1,0:T(8,128)S(1)}, u32[]{:S(2)}, u32[]{:S(2)}) collective-permute-start(f32[1,4,64,64]{3,2,1,0:T(8,128)S(1)} %fusion.109), channel_id=1, source_target_pairs={{0,64},{2,66},{4,68},{6,70},{8,72},{10,74},{12,76},{14,78},{16,80}... | collective-permute-start | bytes 196616 | tf_op jit(solution)/shard_map/ppermute | solution.py:39
  157.0 19.9 %copy-start.6 = (f32[1,128,2,4,64]{1,4,3,2,0:T(8,128)S(1)}, f32[1,128,2,4,64]{1,4,3,2,0:T(8,128)}, u32[]{:S(2)}) copy-start(f32[1,128,2,4,64]{1,4,3,2,0:T(8,128)} %copy-done.5) | copy-start | bytes 786436
  166.7 73.8 %copy-start.9 = (f32[8]{0:T(128)S(1)}, f32[8]{0:T(128)}, u32[]{:S(2)}) copy-start(f32[8]{0:T(128)} %param.23) | copy-start | bytes 100
  166.7 88.1 %copy-start.1 = (bf16[128,256]{1,0:T(8,128)(2,1)S(1)}, bf16[128,256]{1,0:T(8,128)(2,1)}, u32[]{:S(2)}) copy-start(bf16[128,256]{1,0:T(8,128)(2,1)} %param.19) | copy-start | bytes 196612
  179.8 6.5 %collective-permute-start.9 = (f32[2,2,261]{0,2,1:T(8,128)S(1)}, f32[2,2,261]{0,2,1:T(8,128)S(1)}, u32[]{:S(2)}, u32[]{:S(2)}) collective-permute-start(f32[2,2,261]{0,2,1:T(8,128)S(1)} %broadcast_multiply_fusion), channel_id=1, source_target_pairs={{0,1},{1,0},{2,3},{3,2},{4,5},{5,4},{6,7},{7,6},{8,9},{9,8},{10,11... | collective-permute-start | bytes 12536 | tf_op jit(solution)/shard_map/ppermute | solution.py:61
  186.5 8.1 %collective-permute-start.10 = (f32[2,2,261]{0,2,1:T(8,128)S(1)}, f32[2,2,261]{0,2,1:T(8,128)S(1)}, u32[]{:S(2)}, u32[]{:S(2)}) collective-permute-start(f32[2,2,261]{0,2,1:T(8,128)S(1)} %fusion.72), channel_id=1, source_target_pairs={{0,128},{128,0},{1,129},{129,1},{2,130},{130,2},{3,131},{131,3},{4... | collective-permute-start | bytes 12536 | tf_op jit(solution)/shard_map/ppermute | solution.py:61
  194.6 1.6 collective-permute-start.11
  196.3 8.6 %collective-permute-start.12 = (f32[2,2,261]{0,2,1:T(8,128)S(1)}, f32[2,2,261]{0,2,1:T(8,128)S(1)}, u32[]{:S(2)}, u32[]{:S(2)}) collective-permute-start(f32[2,2,261]{0,2,1:T(8,128)S(1)} %add.139), channel_id=1, source_target_pairs={{0,4},{2,6},{4,0},{6,2},{8,12},{10,14},{12,8},{14,10},{16,20},{18,... | collective-permute-start | bytes 12536 | tf_op jit(solution)/shard_map/ppermute | solution.py:61
  204.9 9.3 %collective-permute-start.13 = (f32[2,2,261]{0,2,1:T(8,128)S(1)}, f32[2,2,261]{0,2,1:T(8,128)S(1)}, u32[]{:S(2)}, u32[]{:S(2)}) collective-permute-start(f32[2,2,261]{0,2,1:T(8,128)S(1)} %add.140), channel_id=1, source_target_pairs={{0,8},{2,10},{4,12},{6,14},{8,0},{10,2},{12,4},{14,6},{16,24},{18,... | collective-permute-start | bytes 12536 | tf_op jit(solution)/shard_map/ppermute | solution.py:61
  214.2 7.3 %collective-permute-start.14 = (f32[2,2,261]{0,2,1:T(8,128)S(1)}, f32[2,2,261]{0,2,1:T(8,128)S(1)}, u32[]{:S(2)}, u32[]{:S(2)}) collective-permute-start(f32[2,2,261]{0,2,1:T(8,128)S(1)} %add.141), channel_id=1, source_target_pairs={{0,16},{2,18},{4,20},{6,22},{8,24},{10,26},{12,28},{14,30},{16,0},... | collective-permute-start | bytes 12536 | tf_op jit(solution)/shard_map/ppermute | solution.py:61
  221.5 12.4 %collective-permute-start.15 = (f32[2,2,261]{0,2,1:T(8,128)S(1)}, f32[2,2,261]{0,2,1:T(8,128)S(1)}, u32[]{:S(2)}, u32[]{:S(2)}) collective-permute-start(f32[2,2,261]{0,2,1:T(8,128)S(1)} %add.142), channel_id=1, source_target_pairs={{0,32},{2,34},{4,36},{6,38},{8,40},{10,42},{12,44},{14,46},{16,48}... | collective-permute-start | bytes 12536 | tf_op jit(solution)/shard_map/ppermute | solution.py:61
  233.9 17.8 %collective-permute-start.16 = (f32[2,2,261]{0,2,1:T(8,128)S(1)}, f32[2,2,261]{0,2,1:T(8,128)S(1)}, u32[]{:S(2)}, u32[]{:S(2)}) collective-permute-start(f32[2,2,261]{0,2,1:T(8,128)S(1)} %add.143), channel_id=1, source_target_pairs={{0,64},{2,66},{4,68},{6,70},{8,72},{10,74},{12,76},{14,78},{16,80}... | collective-permute-start | bytes 12536 | tf_op jit(solution)/shard_map/ppermute | solution.py:61
  (3 other events, 2.3 us)
